TPU v7x, 32 devices: a whole 2x2x4 slice. The times are simulated.
32 devices in a mesh: ctx: 8 (over y, x, core), tp: 4 (over z).
Axes of the slice: x: 2, y: 2, z: 4, core: 2. Of those that a mesh axis runs over, the one named last changes fastest.
Arguments:
- tokens: bfloat16 [4096, 4096], P(('ctx', 'tp')), may hold values from -6 to 6
- spike_query: int32 [4096, 32], P('ctx', 'tp'), may hold values 0 or 1
- spike_key: int32 [4096, 32], P('ctx', 'tp'), may hold values 0 or 1
- qkv_weight: bfloat16 [4096, 3, 4096], P(None, None, 'tp'), may hold values from -0.09375 to 0.09375
- qkv_blocks: int32 [3, 32, 32], P(None, None, 'tp'), may hold values 0 or 1
- out_weight: bfloat16 [4096, 4096], P('tp'), may hold values from -0.09375 to 0.09375
- out_blocks: int32 [32, 32], P('tp'), may hold values 0 or 1
- cotangent: bfloat16 [4096, 4096], P(('ctx', 'tp')), may hold values from -6 to 6
Outputs:
- layer_out: bfloat16 [4096, 4096], P(('ctx', 'tp'))
- token_grad: bfloat16 [4096, 4096], P(('ctx', 'tp'))
- qkv_grad: float32 [4096, 3, 4096], P('ctx', None, 'tp')
- out_grad: float32 [4096, 4096], P('tp', 'ctx')
All inputs are finite; a program needn't handle non-finite values. No bound on the sum of `spike_query` or of `spike_key` or of `qkv_blocks` or of `out_blocks` on one device may be relied on, other than what follows from the above.
Results may differ from a plain program's by a relative error of at most 0.014.
Values may be sent and summed in bfloat16 or wider, within the bound.
No kernel may reach another device: no remote copies, remote signals or barrier semaphores. Data moves between devices by JAX's collectives and lax.ppermute only.
A program may use at most 320 MiB of HBM per device.

v0:
```python
import math
import jax
import jax.numpy as jnp
from jax import lax
from jax.sharding import PartitionSpec as P

BLOCK = 128
EPSILON = 1e-05


def carried_in(value, axis, join, neutral):
    place = lax.axis_index(axis)
    gathered = lax.all_gather(value.astype(jnp.bfloat16), axis)
    state = jnp.zeros_like(value) + jnp.asarray(neutral, value.dtype)

    def carried_one(lap, state):
        return join(state, lax.dynamic_index_in_dim(gathered, lap, 0, False).astype(value.dtype))

    return lax.fori_loop(0, place, carried_one, state)


def entering(value, axis, join, neutral):
    count = lax.axis_size(axis)
    place = lax.axis_index(axis)
    ahead = count - 1 - place
    gathered = lax.all_gather(
        value.astype(jnp.bfloat16 if value.dtype == jnp.float32 else value.dtype), axis
    )
    state = jnp.zeros_like(value) + jnp.asarray(neutral, value.dtype)

    def entering_one(lap, state):
        source = count - 1 - lap
        return join(state, lax.dynamic_index_in_dim(gathered, source, 0, False).astype(value.dtype))

    return lax.fori_loop(0, ahead, entering_one, state)


def expand_blocks(blocks):
    row_blocks, col_blocks = blocks.shape
    spread = jnp.broadcast_to(
        blocks.astype(jnp.bfloat16)[:, None, :, None], (row_blocks, BLOCK, col_blocks, BLOCK)
    )
    return spread.reshape(row_blocks * BLOCK, col_blocks * BLOCK)


def qkv_keep_table(qkv_blocks):
    tables = [expand_blocks(qkv_blocks[projection]) for projection in range(3)]
    return jnp.stack(tables, axis=1)


def add_states(earlier, following):
    return earlier + following


def on_device(
    tokens, spike_query, spike_key, qkv_weight, qkv_blocks, out_weight, out_blocks, cotangent
):
    model_width = tokens.shape[1]
    block_rows = spike_query.shape[0]
    local_heads = spike_query.shape[1]
    features = qkv_weight.shape[2]
    head_width = features // local_heads
    highest = lax.Precision.HIGHEST
    qkv_keep = qkv_keep_table(qkv_blocks).reshape(model_width, 3 * features)
    qkv_used = qkv_weight.reshape(model_width, 3 * features) * qkv_keep
    out_used = out_weight * expand_blocks(out_blocks)
    gathered = lax.all_gather(tokens, "tp", axis=0, tiled=True)
    projected = jnp.dot(gathered, qkv_used, preferred_element_type=jnp.float32).astype(jnp.bfloat16)
    projected = projected.reshape(block_rows, 3, local_heads, head_width)
    query_spikes = spike_query.astype(jnp.bfloat16)[:, :, None]
    key_spikes = spike_key.astype(jnp.bfloat16)[:, :, None]
    query_spiked = projected[:, 0] * query_spikes
    key_spiked = projected[:, 1] * key_spikes
    values = projected[:, 2]
    query_wide = query_spiked.astype(jnp.float32)
    key_wide = key_spiked.astype(jnp.float32)
    local_state = jnp.einsum("shd,she->hde", key_spiked, values, preferred_element_type=jnp.float32)
    zeros_state = jnp.zeros_like(local_state)
    prior_state = carried_in(local_state, "ctx", add_states, zeros_state)
    positions = lax.iota(jnp.int32, block_rows)
    causal_keep = positions[:, None] >= positions[None, :]
    scores = jnp.einsum(
        "thd,shd->hts", query_spiked, key_spiked, preferred_element_type=jnp.float32
    )
    scores = jnp.where(causal_keep, scores, 0.0).astype(jnp.bfloat16)
    mixed_rows = jnp.einsum("hts,she->the", scores, values, preferred_element_type=jnp.float32)
    mixed_rows = mixed_rows + jnp.einsum("thd,hde->the", query_wide, prior_state, precision=highest)
    inv_rms = lax.rsqrt(jnp.mean(mixed_rows * mixed_rows, axis=-1, keepdims=True) + EPSILON)
    normed = mixed_rows * inv_rms
    attended = normed.astype(jnp.bfloat16).reshape(block_rows, features)
    row_piece = attended
    head_sum = lax.psum_scatter(
        jnp.dot(row_piece, out_used, preferred_element_type=jnp.float32).astype(jnp.bfloat16),
        "tp",
        scatter_dimension=0,
        tiled=True,
    ).astype(jnp.float32)
    layer_out = (tokens.astype(jnp.float32) + head_sum).astype(jnp.bfloat16)
    grad_rows = lax.all_gather(cotangent, "tp", axis=0, tiled=True)
    grad_attended = jnp.einsum("tm,fm->tf", grad_rows, out_used, preferred_element_type=jnp.float32)
    grad_attended = grad_attended.reshape(block_rows, local_heads, head_width)
    inner_mean = jnp.mean(grad_attended * normed, axis=-1, keepdims=True)
    grad_mixed = inv_rms * (grad_attended - normed * inner_mean)
    grad_low = grad_mixed.astype(jnp.bfloat16)
    local_adjoint = jnp.einsum("thd,the->hde", query_wide, grad_mixed, precision=highest)
    after_state = entering(local_adjoint, "ctx", add_states, zeros_state)
    adjoint_scores = jnp.einsum(
        "the,she->hts", grad_low, values, preferred_element_type=jnp.float32
    )
    adjoint_scores = jnp.where(causal_keep, adjoint_scores, 0.0).astype(jnp.bfloat16)
    grad_query = jnp.einsum(
        "hts,shd->thd", adjoint_scores, key_spiked, preferred_element_type=jnp.float32
    )
    grad_query = grad_query + jnp.einsum("the,hde->thd", grad_mixed, prior_state, precision=highest)
    grad_key = jnp.einsum(
        "hts,thd->shd", adjoint_scores, query_spiked, preferred_element_type=jnp.float32
    )
    grad_key = grad_key + jnp.einsum(
        "she,hde->shd", values.astype(jnp.float32), after_state, precision=highest
    )
    grad_value = jnp.einsum("hts,the->she", scores, grad_low, preferred_element_type=jnp.float32)
    grad_value = grad_value + jnp.einsum("shd,hde->she", key_wide, after_state, precision=highest)
    grad_proj = jnp.stack(
        [
            (grad_query * query_spikes.astype(jnp.float32)).astype(jnp.bfloat16),
            (grad_key * key_spikes.astype(jnp.float32)).astype(jnp.bfloat16),
            grad_value.astype(jnp.bfloat16),
        ],
        axis=1,
    ).reshape(block_rows, 3 * features)
    row_piece = grad_proj
    token_sum = lax.psum_scatter(
        jnp.einsum("tc,mc->tm", row_piece, qkv_used, preferred_element_type=jnp.float32).astype(
            jnp.bfloat16
        ),
        "tp",
        scatter_dimension=0,
        tiled=True,
    ).astype(jnp.float32)
    token_grad = (cotangent.astype(jnp.float32) + token_sum).astype(jnp.bfloat16)
    out_keep_cols = expand_blocks(jnp.transpose(out_blocks))
    slice_rows = model_width // lax.axis_size("ctx")
    norm_factor = 1.0 / math.sqrt(block_rows * lax.axis_size("ctx"))
    qkv_part = jnp.einsum("tm,tc->mc", gathered, grad_proj, preferred_element_type=jnp.float32)
    qkv_part = qkv_part * qkv_keep
    out_part = jnp.einsum("tm,tf->mf", grad_rows, attended, preferred_element_type=jnp.float32)
    out_part = out_part * out_keep_cols
    weight_sum = lax.psum_scatter(
        jnp.concatenate([qkv_part, out_part], axis=1).astype(jnp.bfloat16),
        "ctx",
        scatter_dimension=0,
        tiled=True,
    ).astype(jnp.float32)
    weight_sum = weight_sum * norm_factor
    qkv_grad = weight_sum[:, : 3 * features].reshape(slice_rows, 3, features)
    out_grad = jnp.transpose(weight_sum[:, 3 * features :])
    return (layer_out, token_grad, qkv_grad, out_grad)


def solution(mesh):
    placed = (
        P(("ctx", "tp"), None),
        P("ctx", "tp"),
        P("ctx", "tp"),
        P(None, None, "tp"),
        P(None, None, "tp"),
        P("tp", None),
        P("tp", None),
        P(("ctx", "tp"), None),
    )
    return jax.shard_map(
        on_device,
        mesh=mesh,
        in_specs=placed,
        out_specs=(
            P(("ctx", "tp"), None),
            P(("ctx", "tp"), None),
            P("ctx", None, "tp"),
            P("tp", "ctx"),
        ),
        check_vma=False,
    )
```

profile of v0, /device:TPU:0, one launch (start us, length us, event | category | flops | bytes accessed | tf_op | source)
XLA Modules:
  0.0 714.5 jit_solution(4649358727200529671)
XLA Ops:
  7.2 0.7 all-gather.7.cloned.1.call-update
  8.0 32.2 %copy.43 = bf16[4096,3,1024]{0,2,1:T(8,128)(2,1)} copy(bf16[4096,3,1024]{2,0,1:T(8,128)(2,1)} %param.15) | data formatting | bytes 50331648 | tf_op args[3]
  40.2 4.5 broadcast_in_dim.22
  44.7 13.3 %stack_reshape.9 = bf16[4096,1,1024]{0,2,1:T(8,128)(2,1)} reshape(bf16[32,128,8,128]{1,0,3,2:T(8,128)(2,1)} %broadcast_in_dim.22) | data formatting | bytes 16777216 | tf_op jit(solution)/shard_map/stack;reshape | solution.py:48
  58.0 4.5 broadcast_in_dim.25
  62.5 13.3 %stack_reshape.10 = bf16[4096,1,1024]{0,2,1:T(8,128)(2,1)} reshape(bf16[32,128,8,128]{1,0,3,2:T(8,128)(2,1)} %broadcast_in_dim.25) | data formatting | bytes 16777216 | tf_op jit(solution)/shard_map/stack;reshape | solution.py:48
  75.8 4.5 broadcast_in_dim.26
  80.3 13.4 %stack_reshape.11 = bf16[4096,1,1024]{0,2,1:T(8,128)(2,1)} reshape(bf16[32,128,8,128]{1,0,3,2:T(8,128)(2,1)} %broadcast_in_dim.26) | data formatting | bytes 16777216 | tf_op jit(solution)/shard_map/stack;reshape | solution.py:48
  93.7 7.8 %constant_dynamic-update-slice_fusion.2 = bf16[4096,3,1024]{0,2,1:T(8,128)(2,1)} fusion(bf16[4096,1,1024]{0,2,1:T(8,128)(2,1)} %stack_reshape.9), kind=kLoop, calls=%fused_computation.51 | loop fusion | bytes 16777216
  101.5 7.7 %constant_dynamic-update-slice_fusion.1 = bf16[4096,3,1024]{0,2,1:T(8,128)(2,1)} fusion(bf16[4096,3,1024]{0,2,1:T(8,128)(2,1)} %constant_dynamic-update-slice_fusion.2, bf16[4096,1,1024]{0,2,1:T(8,128)(2,1)} %stack_reshape.10), kind=kLoop, calls=%fused_computation.50 | loop fusion | bytes 16777216
  109.2 7.8 %constant_dynamic-update-slice_fusion = bf16[4096,3,1024]{0,2,1:T(8,128)(2,1)} fusion(bf16[4096,3,1024]{0,2,1:T(8,128)(2,1)} %constant_dynamic-update-slice_fusion.1, bf16[4096,1,1024]{0,2,1:T(8,128)(2,1)} %stack_reshape.11), kind=kLoop, calls=%fused_computation.49 | loop fusion | bytes 16777216 | tf_op jit(solution)/shard_map/stack | solution.py:48
  117.0 28.6 %mul.82 = bf16[4096,3,1024]{0,2,1:T(8,128)(2,1)} multiply(bf16[4096,3,1024]{0,2,1:T(8,128)(2,1)} %copy.43, bf16[4096,3,1024]{0,2,1:T(8,128)(2,1)} %constant_dynamic-update-slice_fusion) | non-fusion elementwise | flops 12582912 | bytes 75497472 | tf_op jit(solution)/shard_map/mul | solution.py:65
  145.7 18.2 %convolution_convert_fusion.2 = bf16[3072,512]{1,0:T(8,128)(2,1)S(1)} fusion(bf16[4096,3072]{0,1:T(8,128)(2,1)} %bitcast.148, bf16[512,4096]{1,0:T(8,128)(2,1)} %all-gather.7.cloned.1.call-done), kind=kOutput, calls=%fused_computation.13 | convolution fusion | flops 12886474752 | bytes 32505856 | tf_op jit(solution)/shard_map/dot_general | solution.py:68
  163.9 1.5 convolution_convert_fusion.3
  165.4 0.7 all-gather.9.cloned.1.call-update
  166.1 0.2 all-gather.13.cloned.1.call-start
  166.3 0.1 iota_compare_fusion
  166.5 1.4 select_convert_fusion.1
  167.9 2.0 copy-done.4
  169.9 2.8 fusion.12
  172.7 22.8 %all-gather.11.cloned.1.call-done = bf16[64,128,128]{2,1,0:T(8,128)(2,1)} async-done(((bf16[8,128,128]{2,1,0:T(8,128)(2,1)}), bf16[64,128,128]{2,1,0:T(8,128)(2,1)}) %all-gather.11.cloned.1.call-update) | async-done | bytes 2097168 | tf_op jit(solution)/shard_map/all_gather | solution.py:13
  195.5 3.1 fusion.5
  198.6 79.2 %all-gather.9.cloned.1.call-done = bf16[512,4096]{1,0:T(8,128)(2,1)} async-done(((bf16[128,4096]{1,0:T(8,128)(2,1)}), bf16[512,4096]{1,0:T(8,128)(2,1)}) %all-gather.9.cloned.1.call-update) | async-done | bytes 4194320 | tf_op jit(solution)/shard_map/all_gather | solution.py:99
  277.8 1.1 broadcast_in_dim.30
  279.0 12.4 %multiply_reduce_fusion = (f32[512,8]{0,1:T(8,128)S(1)}, f32[1024,512]{1,0:T(8,128)S(1)}) fusion(f32[8,128,512]{2,1,0:T(8,128)S(1)} %get-tuple-element.125, f32[512,8]{0,1:T(8,128)S(1)} %add_rsqrt_fusion, bf16[512,4096]{1,0:T(8,128)(2,1)} %all-gather.9.cloned.1.call-done, bf16[1024,4096]{1,0:T(8,128)(2,1)} %param.17, bf16[128,8,32,128]{3,2,1,0:T(8,128)(2,1)S(1)} %bitcast.145), kind=kOutput, calls=%fused_computation.27 | convolution fusion | flops 4300730368 | bytes 25198592 | tf_op jit(solution)/shard_map/tm,fm->tf/dot_general | solution.py:100
  291.4 3.2 subtract_multiply_fusion
  294.6 3.1 convolution_convert_fusion.4
  297.7 0.3 reduce-scatter.4.cloned.1.call-start
  298.0 13.5 %convolution_convert_fusion.1 = bf16[512,4096]{1,0:T(8,128)(2,1)} fusion(bf16[512,1024]{0,1:T(8,128)(2,1)} %bitcast.160, bf16[1024,4096]{1,0:T(8,128)(2,1)} %param.17, bf16[128,8,32,128]{3,2,1,0:T(8,128)(2,1)} %bitcast.146), kind=kOutput, calls=%fused_computation.12 | convolution fusion | flops 4301258752 | bytes 22020096 | tf_op jit(solution)/shard_map/dot_general | solution.py:93
  311.5 0.0 reduce-scatter.6.cloned.1.call-start
  311.5 2.7 select_convert_fusion
  314.3 1.5 fusion.22
  315.8 2.9 fusion.8
  318.6 2.1 fusion.17
  320.8 0.9 copy-done.5
  321.6 2.1 fusion.13
  323.7 0.6 all-gather.13.cloned.1.call-done
  324.3 8.2 %while.23 = (s32[]{:T(128)}, f32[8,128,128]{2,1,0:T(8,128)S(1)}, s32[]{:T(128)}, bf16[8,8,128,128]{3,2,1,0:T(8,128)(2,1)}, s32[]{:T(128)}, /*index=5*/s32[]{:T(128)}, s32[]{:T(128)}, s32[]{:T(128)}) while((s32[]{:T(128)}, f32[8,128,128]{2,1,0:T(8,128)S(1)}, s32[]{:T(128)}, bf16[8,8,128,128]{3,2,1,0:T(8,128)(2,1)}, s32[]{:T(128)}, ...), condition=%wide.region_6.7_spmd, body=%wide.region_5.6_spmd.sunk | while | flops 262150 | bytes 1310863 | solution.py:35
  324.4 1.2 convert_add_fusion.5
  325.6 1.1 convert_add_fusion.5
  326.7 1.1 convert_add_fusion.5
  327.8 1.1 convert_add_fusion.5
  328.9 1.1 convert_add_fusion.5
  330.0 1.1 convert_add_fusion.5
  331.1 1.1 convert_add_fusion.5
  332.6 3.5 fusion.7
  336.1 2.3 fusion.9
  338.4 0.3 pad_maximum_fusion.1
  338.7 1.6 copy-done.12
  340.4 19.9 %convolution_convert_fusion = bf16[512,4096]{1,0:T(8,128)(2,1)} fusion(bf16[512,3072]{0,1:T(8,128)(2,1)S(1)} %bitcast.162, bf16[4096,3072]{0,1:T(8,128)(2,1)} %bitcast.149), kind=kOutput, calls=%fused_computation.11 | convolution fusion | flops 12886999040 | bytes 32505856 | tf_op jit(solution)/shard_map/tc,mc->tm/dot_general | solution.py:133
  360.3 0.0 reduce-scatter.8.cloned.1.call-start
  360.3 8.0 %broadcast_in_dim.58 = f32[32,128,8,128]{1,0,3,2:T(8,128)} broadcast(f32[32,8]{0,1:T(8,128)S(1)} %get-tuple-element.113), dimensions={0,2} | broadcast | bytes 16778240 | tf_op jit(solution)/shard_map/broadcast_in_dim | solution.py:40
  368.3 15.5 %fusion.1 = bf16[4096,1024]{0,1:T(8,128)(2,1)} fusion(f32[128,8,32,128]{3,2,1,0:T(8,128)} %bitcast.143, bf16[512,1024]{0,1:T(8,128)(2,1)S(1)} %bitcast.161, bf16[512,4096]{1,0:T(8,128)(2,1)S(1)} %copy-done.6), kind=kOutput, calls=%fused_computation.6 | convolution fusion | flops 4303355904 | bytes 30408704 | tf_op jit(solution)/shard_map/tm,tf->mf/dot_general | solution.py:146
  383.8 27.2 %fusion = bf16[4096,3072]{0,1:T(8,128)(2,1)} fusion(bf16[4096,3072]{0,1:T(8,128)(2,1)} %bitcast.144, bf16[512,3072]{0,1:T(8,128)(2,1)} %bitcast.163, bf16[512,4096]{1,0:T(8,128)(2,1)} %all-gather.7.cloned.1.call-done), kind=kOutput, calls=%fused_computation.3 | convolution fusion | flops 12922650624 | bytes 57671680 | tf_op jit(solution)/shard_map/tm,tc->mc/dot_general | solution.py:144
  411.0 24.0 %pad_maximum_fusion = bf16[4096,4096]{0,1:T(8,128)(2,1)} fusion(bf16[4096,1024]{0,1:T(8,128)(2,1)} %fusion.1, bf16[4096,3072]{0,1:T(8,128)(2,1)} %fusion), kind=kLoop, calls=%fused_computation.4 | loop fusion | flops 67108864 | bytes 67108864 | tf_op jit(solution)/shard_map/concatenate | solution.py:149
  435.1 1.1 copy-done.9
  436.2 2.4 add_convert_fusion.2
  438.7 44.7 %reduce-scatter.6.cloned.1.call-done = bf16[128,4096]{1,0:T(8,128)(2,1)} async-done(((bf16[512,4096]{1,0:T(8,128)(2,1)}), bf16[128,4096]{1,0:T(8,128)(2,1)}) %reduce-scatter.6.cloned.1.call-update) | async-done | bytes 1048592 | tf_op jit(solution)/shard_map/reduce_scatter | solution.py:132
  483.4 2.4 add_convert_fusion
  485.8 206.9 %reduce-scatter.8.cloned.1.call-done = bf16[512,4096]{0,1:T(8,128)(2,1)} async-done(((bf16[4096,4096]{0,1:T(8,128)(2,1)}), bf16[512,4096]{0,1:T(8,128)(2,1)}) %reduce-scatter.8.cloned.1.call-update) | async-done | bytes 4194320 | tf_op jit(solution)/shard_map/reduce_scatter | solution.py:148
  692.7 3.4 convert_multiply_fusion.1
  696.1 3.3 slice.41
  699.4 1.5 slice_bitcast_fusion
  700.9 6.6 copy.56
  (49 shorter events, 0.4 us)
Async XLA Ops:
  7.2 138.5 %all-gather.7.cloned.1.call-start = ((), (), s32[]{:S(2)}) async-start(), calls=%async_computation.3 | async-start | bytes 5242880 | tf_op jit(solution)/shard_map/all_gather | solution.py:67
  7.9 32.3 %copy-start.15 = (s32[3,32,8]{1,2,0:T(8,128)S(1)}, s32[3,32,8]{1,2,0:T(8,128)}, u32[]{:S(2)}) copy-start(s32[3,32,8]{1,2,0:T(8,128)} %param.16) | copy-start | bytes 9220
  7.9 187.5 %all-gather.11.cloned.1.call-start = ((), (), s32[]{:S(2)}) async-start(), calls=%async_computation.8 | async-start | bytes 2359296 | tf_op jit(solution)/shard_map/all_gather | solution.py:13
  117.0 28.6 %copy-start.13 = (s32[512,8]{0,1:T(8,128)S(1)}, s32[512,8]{0,1:T(8,128)}, u32[]{:S(2)}) copy-start(s32[512,8]{0,1:T(8,128)} %param.13) | copy-start | bytes 49156
  117.0 28.6 %copy-start.14 = (s32[512,8]{0,1:T(8,128)S(1)}, s32[512,8]{0,1:T(8,128)}, u32[]{:S(2)}) copy-start(s32[512,8]{0,1:T(8,128)} %param.14) | copy-start | bytes 49156
  163.8 4.0 copy-start.1
  163.8 2.6 copy-start.16
  165.4 112.4 %all-gather.9.cloned.1.call-start = ((), (), s32[]{:S(2)}) async-start(), calls=%async_computation.5 | async-start | bytes 5242880 | tf_op jit(solution)/shard_map/all_gather | solution.py:99
  166.1 158.2 %all-gather.13.cloned.1.call-start = ((), (), s32[]{:S(2)}) async-start(), calls=%async_computation.9 | async-start | bytes 2359296 | tf_op jit(solution)/shard_map/all_gather | solution.py:26
  167.9 2.0 copy-start.4
  198.6 80.4 %copy-start.3 = (f32[8,128,512]{2,1,0:T(8,128)}, f32[8,128,512]{2,1,0:T(8,128)S(1)}, u32[]{:S(2)}) copy-start(f32[8,128,512]{2,1,0:T(8,128)S(1)} %get-tuple-element.125) | copy-start | bytes 6291460
  279.0 12.4 %copy-start = (bf16[8,128,32,128]{3,2,1,0:T(8,128)(2,1)}, bf16[8,128,32,128]{3,2,1,0:T(8,128)(2,1)S(1)}, u32[]{:S(2)}) copy-start(bf16[8,128,32,128]{3,2,1,0:T(8,128)(2,1)S(1)} %broadcast_in_dim.30) | copy-start | bytes 25165828
  297.7 137.3 %reduce-scatter.4.cloned.1.call-start = ((), (), s32[]{:S(2)}) async-start(), calls=%async_computation.4 | async-start | bytes 5242880 | tf_op jit(solution)/shard_map/reduce_scatter | solution.py:92
  311.5 171.9 %reduce-scatter.6.cloned.1.call-start = ((), (), s32[]{:S(2)}) async-start(), calls=%async_computation.6 | async-start | bytes 5242880 | tf_op jit(solution)/shard_map/reduce_scatter | solution.py:132
  311.5 2.7 copy-start.2
  318.6 3.0 copy-start.5
  324.3 11.8 %copy-start.7 = (f32[8,128,512]{2,1,0:T(8,128)S(1)}, f32[8,128,512]{2,1,0:T(8,128)}, u32[]{:S(2)}) copy-start(f32[8,128,512]{2,1,0:T(8,128)} %fusion.17) | copy-start | bytes 6291460
  332.5 5.8 copy-start.11
  338.7 1.6 copy-start.12
  360.3 332.4 %reduce-scatter.8.cloned.1.call-start = ((), (), s32[]{:S(2)}) async-start(), calls=%async_computation.7 | async-start | bytes 37748736 | tf_op jit(solution)/shard_map/reduce_scatter | solution.py:148
  360.3 8.0 %copy-start.6 = (bf16[512,4096]{1,0:T(8,128)(2,1)S(1)}, bf16[512,4096]{1,0:T(8,128)(2,1)}, u32[]{:S(2)}) copy-start(bf16[512,4096]{1,0:T(8,128)(2,1)} %all-gather.9.cloned.1.call-done) | copy-start | bytes 12582916
  360.3 8.0 %copy-start.8 = (bf16[512,8,128]{0,2,1:T(8,128)(2,1)S(1)}, bf16[512,8,128]{0,2,1:T(8,128)(2,1)}, u32[]{:S(2)}) copy-start(bf16[512,8,128]{0,2,1:T(8,128)(2,1)} %get-tuple-element.120) | copy-start | bytes 3145732
  435.0 1.2 copy-start.9
  435.0 48.4 %copy-start.10 = (bf16[128,4096]{1,0:T(8,128)(2,1)S(1)}, bf16[128,4096]{1,0:T(8,128)(2,1)}, u32[]{:S(2)}) copy-start(bf16[128,4096]{1,0:T(8,128)(2,1)} %param.19) | copy-start | bytes 3145732
Sparse Core Ops, SparseCore 0:
  9.6 83.4 all-gather.6
  165.5 29.8 all-gather.10
  197.0 80.7 all-gather.8
  297.8 26.4 all-gather.12
  327.0 76.7 reduce-scatter.3
  406.1 77.2 reduce-scatter.5
  486.9 205.7 reduce-scatter.7
where the time goes:
time: 725 us; the launch traced here: 715 us
  waiting for transfers between devices  356 us (49%)
  matrix products  136 us (19%)
  local copies, waits for them, and re-layouts  135 us (19%)
  other arithmetic  72 us (10%)
  between operations  14.7 us (2%)
    reduce_scatter x1, waiting for transfers between devices, on_device(): lax.psum_scatter(jnp.concatenate([qkv_part, out_part], axis=1).astype(jnp...  207 us
    all_gather x1, waiting for transfers between devices, on_device(): grad_rows = lax.all_gather(cotangent, 'tp', axis=0, tiled=True)  79.2 us
    unnamed x38, local copies, waits for them, and re-layouts  60 us
    another operation x4, local copies, waits for them, and re-layouts, qkv_keep_table(): return jnp.stack(tables, axis=1)  47.8 us
    reduce_scatter x1, waiting for transfers between devices, on_device(): lax.psum_scatter(jnp.einsum('tc,mc->tm', row_piece, qkv_used, preferred_e...  44.7 us
    mul x1, other arithmetic, on_device(): qkv_used = qkv_weight.reshape(model_width, 3 * features) * qkv_keep  28.6 us
    dot_general x1, matrix products, on_device(): jnp.einsum('tm,tc->mc', gathered, grad_proj, preferred_element_type=jnp.f...  27.2 us
    concatenate x1, other arithmetic, on_device(): jnp.concatenate([qkv_part, out_part], axis=1).astype(jnp.bfloat16)  24 us
  transfers between devices with their start and end apart: 7, of which 5 were waited for; matrix products, arithmetic and copies ran while one was open for 40% of the time, Pallas kernels for 0%

commit v1 on v0

--- a/solution.py
+++ b/solution.py
@@ -96,7 +96,16 @@
         tiled=True,
     ).astype(jnp.float32)
     layer_out = (tokens.astype(jnp.float32) + head_sum).astype(jnp.bfloat16)
-    grad_rows = lax.all_gather(cotangent, "tp", axis=0, tiled=True)
+    ways = lax.axis_size("tp")
+    up = [(d, (d + 1) % ways) for d in range(ways)]
+    down = [(d, (d - 1) % ways) for d in range(ways)]
+    earlier_2, later = ([cotangent], [cotangent])
+    for _ in range(ways // 2):
+        earlier_2.append(lax.ppermute(earlier_2[-1], "tp", up))
+    for _ in range((ways - 1) // 2):
+        later.append(lax.ppermute(later[-1], "tp", down))
+    line = jnp.concatenate([*earlier_2[::-1], *later[1:]], axis=0)
+    grad_rows = jnp.roll(line, (lax.axis_index("tp") - ways // 2) * cotangent.shape[0], axis=0)
     grad_attended = jnp.einsum("tm,fm->tf", grad_rows, out_used, preferred_element_type=jnp.float32)
     grad_attended = grad_attended.reshape(block_rows, local_heads, head_width)
     inner_mean = jnp.mean(grad_attended * normed, axis=-1, keepdims=True)

time: 725 us -> 665 us (0.917)
  waiting for transfers between devices: 356 us -> 270 us
  local copies, waits for them, and re-layouts: 135 us -> 149 us
  matrix products: 136 us -> 144 us
    all_gather x1 -> x0, waiting for transfers between devices: 79.2 us -> none  [on_device(): grad_rows = lax.all_gather(cotangent, 'tp', axis=0, tiled=True)]
    all_gather x1, waiting for transfers between devices: 22.8 us -> 10.4 us  [carried_in(): gathered = lax.all_gather(value.astype(jnp.bfloat16), axis)]
    unnamed x38 -> x49, local copies, waits for them, and re-layouts: 60 us -> 71.3 us
    all_gather x1, waiting for transfers between devices: 0.59 us -> 9.59 us  [entering(): lax.all_gather(value.astype(jnp.bfloat16 if value.dtype == jnp.float32 el...]
  transfers between devices with their start and end apart: 7 -> 9, of which waited for: 5 -> 4; matrix products, arithmetic and copies ran while one was open for 40% -> 48% of each run, Pallas kernels for 0% -> 0%
where the time goes in v1:
time: 665 us; the launch traced here: 657 us
  waiting for transfers between devices  270 us (41%)
  local copies, waits for them, and re-layouts  149 us (22%)
  matrix products  144 us (22%)
  other arithmetic  72.3 us (11%)
  between operations  14.7 us (2%)
    reduce_scatter x1, waiting for transfers between devices, on_device(): lax.psum_scatter(jnp.concatenate([qkv_part, out_part], axis=1).astype(jnp...  207 us
    unnamed x49, local copies, waits for them, and re-layouts  71.3 us
    another operation x4, local copies, waits for them, and re-layouts, qkv_keep_table(): return jnp.stack(tables, axis=1)  48 us
    reduce_scatter x1, waiting for transfers between devices, on_device(): lax.psum_scatter(jnp.einsum('tc,mc->tm', row_piece, qkv_used, preferred_e...  42.8 us
    mul x1, other arithmetic, on_device(): qkv_used = qkv_weight.reshape(model_width, 3 * features) * qkv_keep  28.6 us
    dot_general x1, matrix products, on_device(): jnp.einsum('tm,tc->mc', gathered, grad_proj, preferred_element_type=jnp.f...  25.8 us
    concatenate x1, other arithmetic, on_device(): jnp.concatenate([qkv_part, out_part], axis=1).astype(jnp.bfloat16)  23.5 us
    broadcast_in_dim x5, local copies, waits for them, and re-layouts, expand_blocks(): jnp.broadcast_to(blocks.astype(jnp.bfloat16)[:, None, :, None], (row_bloc...  22.3 us
  transfers between devices with their start and end apart: 9, of which 4 were waited for; matrix products, arithmetic and copies ran while one was open for 48% of the time, Pallas kernels for 0%

profile of v1, /device:TPU:0, one launch (start us, length us, event | category | flops | bytes accessed | tf_op | source)
XLA Modules:
  0.0 657.1 jit_solution(11349173817752734382)
XLA Ops:
  7.9 3.1 collective-permute-start
  11.0 2.1 collective-permute-start.2
  13.1 33.6 %copy.45 = bf16[4096,3,1024]{0,2,1:T(8,128)(2,1)} copy(bf16[4096,3,1024]{2,0,1:T(8,128)(2,1)} %param.15) | data formatting | bytes 50331648 | tf_op args[3]
  46.7 4.4 broadcast_in_dim.22
  51.1 13.3 %stack_reshape.9 = bf16[4096,1,1024]{0,2,1:T(8,128)(2,1)} reshape(bf16[32,128,8,128]{1,0,3,2:T(8,128)(2,1)} %broadcast_in_dim.22) | data formatting | bytes 16777216 | tf_op jit(solution)/shard_map/stack;reshape | solution.py:48
  64.5 4.4 broadcast_in_dim.25
  68.8 13.3 %stack_reshape.10 = bf16[4096,1,1024]{0,2,1:T(8,128)(2,1)} reshape(bf16[32,128,8,128]{1,0,3,2:T(8,128)(2,1)} %broadcast_in_dim.25) | data formatting | bytes 16777216 | tf_op jit(solution)/shard_map/stack;reshape | solution.py:48
  82.2 4.4 broadcast_in_dim.26
  86.6 13.3 %stack_reshape.11 = bf16[4096,1,1024]{0,2,1:T(8,128)(2,1)} reshape(bf16[32,128,8,128]{1,0,3,2:T(8,128)(2,1)} %broadcast_in_dim.26) | data formatting | bytes 16777216 | tf_op jit(solution)/shard_map/stack;reshape | solution.py:48
  99.9 7.7 %constant_dynamic-update-slice_fusion.2 = bf16[4096,3,1024]{0,2,1:T(8,128)(2,1)} fusion(bf16[4096,1,1024]{0,2,1:T(8,128)(2,1)} %stack_reshape.9), kind=kLoop, calls=%fused_computation.52 | loop fusion | bytes 16777216
  107.6 7.7 %constant_dynamic-update-slice_fusion.1 = bf16[4096,3,1024]{0,2,1:T(8,128)(2,1)} fusion(bf16[4096,3,1024]{0,2,1:T(8,128)(2,1)} %constant_dynamic-update-slice_fusion.2, bf16[4096,1,1024]{0,2,1:T(8,128)(2,1)} %stack_reshape.10), kind=kLoop, calls=%fused_computation.51 | loop fusion | bytes 16777216
  115.6 8.0 %constant_dynamic-update-slice_fusion = bf16[4096,3,1024]{0,2,1:T(8,128)(2,1)} fusion(bf16[4096,3,1024]{0,2,1:T(8,128)(2,1)} %constant_dynamic-update-slice_fusion.1, bf16[4096,1,1024]{0,2,1:T(8,128)(2,1)} %stack_reshape.11), kind=kLoop, calls=%fused_computation.50 | loop fusion | bytes 16777216 | tf_op jit(solution)/shard_map/stack | solution.py:48
  123.6 28.6 %mul.85 = bf16[4096,3,1024]{0,2,1:T(8,128)(2,1)} multiply(bf16[4096,3,1024]{0,2,1:T(8,128)(2,1)} %copy.45, bf16[4096,3,1024]{0,2,1:T(8,128)(2,1)} %constant_dynamic-update-slice_fusion) | non-fusion elementwise | flops 12582912 | bytes 75497472 | tf_op jit(solution)/shard_map/mul | solution.py:65
  152.4 1.2 constant_dynamic-update-slice_fusion.10
  153.7 18.2 %convolution_convert_fusion.2 = bf16[3072,512]{1,0:T(8,128)(2,1)S(1)} fusion(bf16[4096,3072]{0,1:T(8,128)(2,1)} %bitcast.142, bf16[512,4096]{1,0:T(8,128)(2,1)} %all-gather.6.cloned.1.call-done), kind=kOutput, calls=%fused_computation.13 | convolution fusion | flops 12886474752 | bytes 32505856 | tf_op jit(solution)/shard_map/dot_general | solution.py:68
  171.9 1.5 convolution_convert_fusion.3
  173.5 2.5 constant_dynamic-update-slice_fusion.9
  175.9 2.4 constant_dynamic-update-slice_fusion.8
  178.3 2.3 constant_dynamic-update-slice_fusion.7
  180.7 1.1 constant_dynamic-update-slice_fusion.6
  181.7 1.1 constant_dynamic-update-slice_fusion.5
  182.8 1.1 constant_dynamic-update-slice_fusion.4
  183.9 2.3 constant_dynamic-update-slice_fusion.3
  186.2 1.4 select_convert_fusion.1
  187.6 2.0 copy-done.3
  189.6 2.8 fusion.14
  192.4 10.4 %all-gather.8.cloned.1.call-done = bf16[64,128,128]{2,1,0:T(8,128)(2,1)} async-done(((bf16[8,128,128]{2,1,0:T(8,128)(2,1)}), bf16[64,128,128]{2,1,0:T(8,128)(2,1)}) %all-gather.8.cloned.1.call-update) | async-done | bytes 2097168 | tf_op jit(solution)/shard_map/all_gather | solution.py:13
  203.1 4.4 fusion.7
  207.5 1.1 broadcast_in_dim.30
  208.6 15.7 %multiply_reduce_fusion = (f32[512,8]{0,1:T(8,128)S(1)}, f32[512,1024]{0,1:T(8,128)}) fusion(f32[8,128,512]{2,1,0:T(8,128)} %get-tuple-element.125, f32[512,8]{0,1:T(8,128)S(1)} %add_rsqrt_fusion, bf16[1024,4096]{1,0:T(8,128)(2,1)} %param.17, bf16[128,8,32,128]{3,2,1,0:T(8,128)(2,1)S(1)} %bitcast.139, ...), kind=kOutput, calls=%fused_computation.29 | convolution fusion | flops 4300730368 | bytes 25198596 | tf_op jit(solution)/shard_map/tm,fm->tf/dot_general | solution.py:109
  224.3 3.9 subtract_multiply_fusion
  228.2 3.1 convolution_convert_fusion.4
  231.8 13.3 %convolution_convert_fusion.1 = bf16[512,4096]{1,0:T(8,128)(2,1)} fusion(bf16[512,1024]{0,1:T(8,128)(2,1)} %bitcast.154, bf16[1024,4096]{1,0:T(8,128)(2,1)} %param.17, bf16[128,8,32,128]{3,2,1,0:T(8,128)(2,1)} %bitcast.140), kind=kOutput, calls=%fused_computation.12 | convolution fusion | flops 4301258752 | bytes 22020096 | tf_op jit(solution)/shard_map/dot_general | solution.py:93
  245.2 2.8 select_convert_fusion
  248.0 1.5 fusion.24
  249.5 2.9 fusion.10
  252.3 2.1 fusion.19
  254.5 0.8 copy-done.4
  255.3 2.0 fusion.15
  257.3 9.6 %all-gather.10.cloned.1.call-done = bf16[64,128,128]{2,1,0:T(8,128)(2,1)} async-done(((bf16[8,128,128]{2,1,0:T(8,128)(2,1)}), bf16[64,128,128]{2,1,0:T(8,128)(2,1)}) %all-gather.10.cloned.1.call-update) | async-done | bytes 2097168 | tf_op jit(solution)/shard_map/all_gather | solution.py:26
  267.0 8.0 %while.23 = (s32[]{:T(128)}, f32[8,128,128]{2,1,0:T(8,128)S(1)}, s32[]{:T(128)}, bf16[8,8,128,128]{3,2,1,0:T(8,128)(2,1)}, s32[]{:T(128)}, /*index=5*/s32[]{:T(128)}, s32[]{:T(128)}, s32[]{:T(128)}) while((s32[]{:T(128)}, f32[8,128,128]{2,1,0:T(8,128)S(1)}, s32[]{:T(128)}, bf16[8,8,128,128]{3,2,1,0:T(8,128)(2,1)}, s32[]{:T(128)}, ...), condition=%wide.region_6.7_spmd, body=%wide.region_5.6_spmd.sunk | while | flops 262150 | bytes 1310863 | solution.py:35
  267.0 1.2 convert_add_fusion.5
  268.2 1.1 convert_add_fusion.5
  269.3 1.1 convert_add_fusion.5
  270.4 1.1 convert_add_fusion.5
  271.5 1.1 convert_add_fusion.5
  272.6 1.1 convert_add_fusion.5
  273.7 1.1 convert_add_fusion.5
  275.0 3.6 fusion.9
  278.6 2.3 fusion.11
  281.2 19.5 %convolution_convert_fusion = bf16[512,4096]{1,0:T(8,128)(2,1)} fusion(bf16[512,3072]{0,1:T(8,128)(2,1)S(1)} %bitcast.156, bf16[4096,3072]{0,1:T(8,128)(2,1)} %bitcast.143), kind=kOutput, calls=%fused_computation.11 | convolution fusion | flops 12886999040 | bytes 32505856 | tf_op jit(solution)/shard_map/tc,mc->tm/dot_general | solution.py:142
  301.1 8.0 %broadcast_in_dim.58 = f32[32,128,8,128]{1,0,3,2:T(8,128)} broadcast(f32[32,8]{0,1:T(8,128)S(1)} %get-tuple-element.113), dimensions={0,2} | broadcast | bytes 16778240 | tf_op jit(solution)/shard_map/broadcast_in_dim | solution.py:40
  309.0 21.2 %fusion.1 = bf16[4096,1024]{0,1:T(8,128)(2,1)} fusion(f32[128,8,32,128]{3,2,1,0:T(8,128)} %bitcast.137, bf16[512,1024]{0,1:T(8,128)(2,1)S(1)} %bitcast.155, bf16[1024,4096]{1,0:T(8,128)(2,1)} %constant_dynamic-update-slice_fusion.3, s32[]{:T(128)S(6)} %select_n.33), kind=kOutput, calls=%fused_computation.6 | convolution fusion | flops 4303355904 | bytes 30408708 | tf_op jit(solution)/shard_map/tm,tf->mf/dot_general | solution.py:155
  330.2 25.8 %fusion = bf16[4096,3072]{0,1:T(8,128)(2,1)} fusion(bf16[4096,3072]{0,1:T(8,128)(2,1)} %bitcast.138, bf16[512,3072]{0,1:T(8,128)(2,1)S(1)} %bitcast.157, bf16[512,4096]{1,0:T(8,128)(2,1)} %all-gather.6.cloned.1.call-done), kind=kOutput, calls=%fused_computation.3 | convolution fusion | flops 12922650624 | bytes 57671680 | tf_op jit(solution)/shard_map/tm,tc->mc/dot_general | solution.py:153
  356.0 23.5 %pad_maximum_fusion = bf16[4096,4096]{0,1:T(8,128)(2,1)} fusion(bf16[4096,1024]{0,1:T(8,128)(2,1)} %fusion.1, bf16[4096,3072]{0,1:T(8,128)(2,1)} %fusion), kind=kLoop, calls=%fused_computation.4 | loop fusion | flops 67108864 | bytes 67108864 | tf_op jit(solution)/shard_map/concatenate | solution.py:158
  379.6 1.1 copy-done.9
  380.8 2.4 add_convert_fusion.2
  383.2 42.8 %reduce-scatter.6.cloned.1.call-done = bf16[128,4096]{1,0:T(8,128)(2,1)} async-done(((bf16[512,4096]{1,0:T(8,128)(2,1)}), bf16[128,4096]{1,0:T(8,128)(2,1)}) %reduce-scatter.6.cloned.1.call-update) | async-done | bytes 1048592 | tf_op jit(solution)/shard_map/reduce_scatter | solution.py:141
  426.0 2.4 add_convert_fusion
  428.4 206.8 %reduce-scatter.8.cloned.1.call-done = bf16[512,4096]{0,1:T(8,128)(2,1)} async-done(((bf16[4096,4096]{0,1:T(8,128)(2,1)}), bf16[512,4096]{0,1:T(8,128)(2,1)}) %reduce-scatter.8.cloned.1.call-update) | async-done | bytes 4194320 | tf_op jit(solution)/shard_map/reduce_scatter | solution.py:157
  635.2 3.4 convert_multiply_fusion.1
  638.6 3.4 slice.41
  641.9 1.5 slice_bitcast_fusion
  643.4 6.6 copy.59
  (64 shorter events, 2.7 us)
Async XLA Ops:
  7.2 146.4 %all-gather.6.cloned.1.call-start = ((), (), s32[]{:S(2)}) async-start(), calls=%async_computation.3 | async-start | bytes 5242880 | tf_op jit(solution)/shard_map/all_gather | solution.py:67
  7.9 194.9 %all-gather.8.cloned.1.call-start = ((), (), s32[]{:S(2)}) async-start(), calls=%async_computation.7 | async-start | bytes 2359296 | tf_op jit(solution)/shard_map/all_gather | solution.py:13
  7.9 107.4 %collective-permute-start = (bf16[128,4096]{1,0:T(8,128)(2,1)}, bf16[128,4096]{1,0:T(8,128)(2,1)S(1)}, u32[]{:S(2)}, u32[]{:S(2)}) collective-permute-start(bf16[128,4096]{1,0:T(8,128)(2,1)} %param.19), channel_id=1, source_target_pairs={{0,1},{1,2},{2,3},{3,0},{4,5},{5,6},{6,7},{7,4},{8,9},{9,10},{10,1... | collective-permute-start | bytes 3145736 | tf_op jit(solution)/shard_map/ppermute | solution.py:104
  11.0 167.3 %collective-permute-start.2 = (bf16[128,4096]{1,0:T(8,128)(2,1)}, bf16[128,4096]{1,0:T(8,128)(2,1)}, u32[]{:S(2)}, u32[]{:S(2)}) collective-permute-start(bf16[128,4096]{1,0:T(8,128)(2,1)} %param.19), channel_id=1, source_target_pairs={{0,3},{1,0},{2,1},{3,2},{4,7},{5,4},{6,5},{7,6},{8,11},{9,8},{10,9... | collective-permute-start | bytes 3145736 | tf_op jit(solution)/shard_map/ppermute | solution.py:106
  13.1 33.6 %copy-start.17 = (s32[3,32,8]{1,2,0:T(8,128)S(1)}, s32[3,32,8]{1,2,0:T(8,128)}, u32[]{:S(2)}) copy-start(s32[3,32,8]{1,2,0:T(8,128)} %param.16) | copy-start | bytes 9220
  115.4 8.2 %copy-start.10 = (bf16[128,4096]{1,0:T(8,128)(2,1)}, bf16[128,4096]{1,0:T(8,128)(2,1)S(1)}, u32[]{:S(2)}) copy-start(bf16[128,4096]{1,0:T(8,128)(2,1)S(1)} %collective-permute-done) | copy-start | bytes 3145732
  115.4 37.0 %collective-permute-start.1 = (bf16[128,4096]{1,0:T(8,128)(2,1)S(1)}, bf16[128,4096]{1,0:T(8,128)(2,1)S(1)}, u32[]{:S(2)}, u32[]{:S(2)}) collective-permute-start(bf16[128,4096]{1,0:T(8,128)(2,1)S(1)} %collective-permute-done), channel_id=1, source_target_pairs={{0,1},{1,2},{2,3},{3,0},{4,5},{5,6},{6,7},{7,4},{8,9},{9,10},{10,1... | collective-permute-start | bytes 3145736 | tf_op jit(solution)/shard_map/ppermute | solution.py:104
  123.6 28.7 %copy-start.18 = (s32[8,32]{1,0:T(8,128)S(1)}, s32[8,32]{1,0:T(8,128)}, u32[]{:S(2)}) copy-start(s32[8,32]{1,0:T(8,128)} %param.18) | copy-start | bytes 3076
  123.6 28.7 %copy-start.15 = (s32[512,8]{0,1:T(8,128)S(1)}, s32[512,8]{0,1:T(8,128)}, u32[]{:S(2)}) copy-start(s32[512,8]{0,1:T(8,128)} %param.13) | copy-start | bytes 49156
  123.6 28.8 %copy-start.16 = (s32[512,8]{0,1:T(8,128)S(1)}, s32[512,8]{0,1:T(8,128)}, u32[]{:S(2)}) copy-start(s32[512,8]{0,1:T(8,128)} %param.14) | copy-start | bytes 49156
  152.4 1.3 copy-start.12
  171.9 15.7 %copy-start.1 = (bf16[3072,512]{1,0:T(8,128)(2,1)}, bf16[3072,512]{1,0:T(8,128)(2,1)S(1)}, u32[]{:S(2)}) copy-start(bf16[3072,512]{1,0:T(8,128)(2,1)S(1)} %convolution_convert_fusion.2) | copy-start | bytes 9437188
  173.4 93.5 %all-gather.10.cloned.1.call-start = ((), (), s32[]{:S(2)}) async-start(), calls=%async_computation.8 | async-start | bytes 2359296 | tf_op jit(solution)/shard_map/all_gather | solution.py:26
  173.4 7.2 %copy-start.13 = (bf16[128,4096]{1,0:T(8,128)(2,1)S(1)}, bf16[128,4096]{1,0:T(8,128)(2,1)}, u32[]{:S(2)}) copy-start(bf16[128,4096]{1,0:T(8,128)(2,1)} %copy-done.12) | copy-start | bytes 3145732
  173.5 8.3 %copy-start.11 = (bf16[128,4096]{1,0:T(8,128)(2,1)S(1)}, bf16[128,4096]{1,0:T(8,128)(2,1)}, u32[]{:S(2)}) copy-start(bf16[128,4096]{1,0:T(8,128)(2,1)} %copy-done.10) | copy-start | bytes 3145732
  175.9 6.8 %copy-start.5 = (bf16[128,4096]{1,0:T(8,128)(2,1)S(1)}, bf16[128,4096]{1,0:T(8,128)(2,1)}, u32[]{:S(2)}) copy-start(bf16[128,4096]{1,0:T(8,128)(2,1)} %param.19) | copy-start | bytes 3145732
  187.6 2.0 copy-start.3
  208.6 15.7 %copy-start = (bf16[8,128,32,128]{3,2,1,0:T(8,128)(2,1)}, bf16[8,128,32,128]{3,2,1,0:T(8,128)(2,1)S(1)}, u32[]{:S(2)}) copy-start(bf16[8,128,32,128]{3,2,1,0:T(8,128)(2,1)S(1)} %broadcast_in_dim.30) | copy-start | bytes 25165828
  231.4 148.3 %reduce-scatter.4.cloned.1.call-start = ((), (), s32[]{:S(2)}) async-start(), calls=%async_computation.4 | async-start | bytes 5242880 | tf_op jit(solution)/shard_map/reduce_scatter | solution.py:92
  245.1 180.8 %reduce-scatter.6.cloned.1.call-start = ((), (), s32[]{:S(2)}) async-start(), calls=%async_computation.5 | async-start | bytes 5242880 | tf_op jit(solution)/shard_map/reduce_scatter | solution.py:141
  245.2 2.8 copy-start.2
  252.3 2.9 copy-start.4
  267.0 11.6 %copy-start.7 = (f32[8,128,512]{2,1,0:T(8,128)S(1)}, f32[8,128,512]{2,1,0:T(8,128)}, u32[]{:S(2)}) copy-start(f32[8,128,512]{2,1,0:T(8,128)} %fusion.19) | copy-start | bytes 6291460
  275.0 5.9 copy-start.14
  300.8 334.4 %reduce-scatter.8.cloned.1.call-start = ((), (), s32[]{:S(2)}) async-start(), calls=%async_computation.6 | async-start | bytes 37748736 | tf_op jit(solution)/shard_map/reduce_scatter | solution.py:157
  301.1 8.0 %copy-start.8 = (bf16[512,8,128]{0,2,1:T(8,128)(2,1)S(1)}, bf16[512,8,128]{0,2,1:T(8,128)(2,1)}, u32[]{:S(2)}) copy-start(bf16[512,8,128]{0,2,1:T(8,128)(2,1)} %get-tuple-element.120) | copy-start | bytes 3145732
  379.6 1.2 copy-start.9
  379.6 46.4 %copy-start.6 = (bf16[128,4096]{1,0:T(8,128)(2,1)S(1)}, bf16[128,4096]{1,0:T(8,128)(2,1)}, u32[]{:S(2)}) copy-start(bf16[128,4096]{1,0:T(8,128)(2,1)} %param.19) | copy-start | bytes 3145732
Sparse Core Ops, SparseCore 0:
  9.6 123.7 all-gather.5
  173.5 29.2 all-gather.7
  231.5 35.4 all-gather.9
  269.6 76.7 reduce-scatter.3
  348.7 77.2 reduce-scatter.5
  429.4 205.7 reduce-scatter.7
